TPU v7x, 256 devices: a whole 4x4x8 slice. The times are simulated.
256 devices in a mesh: ch: 64 (over z_lo, y, x), ta: 4 (over z_hi, core).
Axes of the slice: x: 4, y: 4, z: 8 (z_hi: 2, z_lo: 4; z = z_hi * 4 + z_lo), core: 2. Of those that a mesh axis runs over, the one named last changes fastest.
Arguments:
- raw: bfloat16 [16384, 20480], P('ch', 'ta'), may hold values from -40 to 40
- fir_taps: bfloat16 [129], replicated, may hold values from -0.5 to 0.5
- start_basis: float32 [512, 16], replicated, may hold values from -6 to 6
Outputs:
- cleaned: bfloat16 [16384, 20480], P('ch', 'ta')
All inputs are finite; a program needn't handle non-finite values.
Results may differ from a plain program's by a relative error of at most 0.008.
Values may be sent and summed in bfloat16 or wider, within the bound.
No kernel may reach another device: no remote copies, remote signals or barrier semaphores. Data moves between devices by JAX's collectives and lax.ppermute only.
A program may use at most 64 MiB of HBM per device.

v0:
```python
import math
import jax
import jax.numpy as jnp
from jax import lax
from jax.sharding import PartitionSpec as P

TAPS = 129
GAUGE = 4
STRIDE = 128
RANK = 16
ITERS = 6
WIN = 512


def with_halo(block, sides, width):
    for axis, dim in sides:
        count = lax.axis_size(axis)
        forward = [(i, i + 1) for i in range(count - 1)]
        backward = [(target, source) for source, target in forward]
        low = lax.ppermute(
            lax.slice_in_dim(block, block.shape[dim] - width, None, axis=dim), axis, forward
        )
        high = lax.ppermute(lax.slice_in_dim(block, 0, width, axis=dim), axis, backward)
        block = jnp.concatenate([low, block, high], axis=dim)
    return block


def shifted(value, axis, steps):
    count = lax.axis_size(axis)
    first, last = (max(0, -steps), min(count, count - steps))
    return lax.ppermute(value, axis, [(source, source + steps) for source in range(first, last)])


def toeplitz_band(taps, width):
    count = taps.shape[0]
    line = jnp.concatenate([taps, jnp.zeros((width,), taps.dtype)])
    flat = jnp.tile(line, width)[: width * (count + width - 1)]
    return flat.reshape(width, count + width - 1).T


def orthonormal(image):
    gram = jnp.einsum("wcr,wcs->wrs", image, image, precision=lax.Precision.HIGHEST)
    lower = jnp.linalg.cholesky(gram)
    return lax.linalg.triangular_solve(lower, image, left_side=False, lower=True, transpose_a=True)


def per_device(raw, fir_taps, start_basis):
    chans = raw.shape[0]
    samples = raw.shape[1]
    half = (TAPS - 1) // 2
    width = math.gcd(samples, 256)
    padded = with_halo(raw, (("ta", 1),), half)
    band_matrix = toeplitz_band(fir_taps, width)
    pieces = jnp.stack(
        [
            padded[:, number * width : number * width + width + TAPS - 1]
            for number in range(samples // width)
        ]
    )
    filtered = jnp.einsum(
        "bct,tu->cbu", pieces, band_matrix, preferred_element_type=jnp.float32
    ).reshape(chans, samples)
    extended = with_halo(filtered, (("ch", 0),), GAUGE)
    gauged = (extended[2 * GAUGE :] - extended[: -2 * GAUGE]).astype(jnp.bfloat16)
    lower_part = shifted(gauged, "ch", 1)
    upper_part = shifted(gauged[:STRIDE], "ch", -1)
    stacked = jnp.concatenate([lower_part, gauged, upper_part], axis=0)
    windows = chans // STRIDE
    total_time = samples * lax.axis_size("ta")
    basis = jnp.broadcast_to(start_basis, (windows, WIN, RANK))
    partial_mats = jnp.stack(
        [
            jnp.dot(
                stacked[number * STRIDE : number * STRIDE + WIN],
                stacked[number * STRIDE : number * STRIDE + WIN].T,
                preferred_element_type=jnp.float32,
            )
            for number in range(windows)
        ]
    )
    scatter_mat = lax.psum(partial_mats, "ta") / total_time
    for sweep in range(ITERS):
        basis = orthonormal(
            jnp.einsum("wcd,wdr->wcr", scatter_mat, basis, precision=lax.Precision.HIGHEST)
        )
    rounded = basis.astype(jnp.bfloat16)
    outputs = []
    for number in range(windows):
        frame = stacked[number * STRIDE : number * STRIDE + WIN]
        coeffs = jnp.dot(rounded[number].T, frame, preferred_element_type=jnp.float32).astype(
            jnp.bfloat16
        )
        fitted = jnp.dot(
            rounded[number, 2 * STRIDE : 3 * STRIDE], coeffs, preferred_element_type=jnp.float32
        )
        outputs.append(
            (frame[2 * STRIDE : 3 * STRIDE].astype(jnp.float32) - fitted).astype(jnp.bfloat16)
        )
    return jnp.concatenate(outputs, axis=0)


def solution(mesh):
    return jax.shard_map(
        per_device,
        mesh=mesh,
        in_specs=(P("ch", "ta"), P(), P()),
        out_specs=P("ch", "ta"),
        check_vma=False,
    )
```

profile of v0, /device:TPU:1, one launch (start us, length us, event | category | flops | bytes accessed | tf_op | source)
XLA Modules:
  0.0 292.5 jit_solution(11654293994104194249)
XLA Ops:
  7.7 10.2 %collective-permute-start = (bf16[256,64]{1,0:T(8,128)(2,1)S(1)}, bf16[256,64]{1,0:T(8,128)(2,1)S(1)}, u32[]{:S(2)}, u32[]{:S(2)}) collective-permute-start(bf16[256,64]{1,0:T(8,128)(2,1)S(1)} %get-tuple-element.10), channel_id=1, source_target_pairs={{0,1},{1,2},{2,3},{4,5},{5,6},{6,7},{8,9},{9,10},{10,11},{12,13},{... | collective-permute-start | bytes 98312 | tf_op jit(solution)/shard_map/ppermute | solution.py:20
  24.8 2.6 collective-permute-done.1
  32.8 4.0 %collective-permute-start.3 = (f32[4,5120]{1,0:T(4,128)S(1)}, f32[4,5120]{1,0:T(4,128)S(1)}, u32[]{:S(2)}, u32[]{:S(2)}) collective-permute-start(f32[4,5120]{1,0:T(4,128)S(1)} %bitcast.161), channel_id=1, source_target_pairs={{0,4},{4,8},{8,12},{12,16},{16,20},{20,24},{24,28},{28,32},{32,36}... | collective-permute-start | bytes 245768 | tf_op jit(solution)/shard_map/ppermute | solution.py:20
  36.8 5.9 %copy.21 = f32[256,20,256]{0,2,1:T(8,128)} copy(f32[256,20,256]{2,0,1:T(8,128)} %copy-done.3) | data formatting | bytes 10485760 | tf_op jit(solution)/shard_map/bct,tu->cbu/transpose | solution.py:60
  42.7 5.9 %copy.22 = f32[256,5120]{1,0:T(8,128)} copy(f32[256,5120]{0,1:T(8,128)} %bitcast.160) | data formatting | bytes 10485760 | tf_op jit(solution)/shard_map/reshape | solution.py:62
  48.6 4.7 %fusion.3 = bf16[256,5120]{1,0:T(8,128)(2,1)S(1)} fusion(f32[256,5120]{1,0:T(8,128)} %copy.22, f32[4,5120]{1,0:T(4,128)S(1)} %collective-permute-done.3, f32[4,5120]{1,0:T(4,128)S(1)} %collective-permute-done.2), kind=kLoop, calls=%fused_computation.10 | loop fusion | flops 5242880 | bytes 8028160 | tf_op jit(solution)/shard_map/convert_element_type | solution.py:64
  53.3 3.3 %collective-permute-start.4 = (bf16[256,5120]{1,0:T(8,128)(2,1)S(1)}, bf16[256,5120]{1,0:T(8,128)(2,1)S(1)}, u32[]{:S(2)}, u32[]{:S(2)}) collective-permute-start(bf16[256,5120]{1,0:T(8,128)(2,1)S(1)} %fusion.3), channel_id=1, source_target_pairs={{0,4},{4,8},{8,12},{12,16},{16,20},{20,24},{24,28},{28,32},{32,36}... | collective-permute-start | bytes 7864328 | tf_op jit(solution)/shard_map/ppermute | solution.py:31
  58.2 49.6 %collective-permute-done.4 = bf16[256,5120]{1,0:T(8,128)(2,1)S(1)} collective-permute-done((bf16[256,5120]{1,0:T(8,128)(2,1)S(1)}, bf16[256,5120]{1,0:T(8,128)(2,1)S(1)}, u32[]{:S(2)}, u32[]{:S(2)}) %collective-permute-start.4) | collective-permute-done | bytes 2621472 | tf_op jit(solution)/shard_map/ppermute | solution.py:31
  107.8 2.9 fusion.19
  110.8 2.9 fusion.18
  115.3 105.3 %all-reduce.3.cloned.1.call-done = f32[2,512,512]{2,1,0:T(8,128)} async-done(((f32[2,512,512]{2,1,0:T(8,128)}), f32[2,512,512]{2,1,0:T(8,128)}) %all-reduce.3.cloned.1.call-update) | async-done | bytes 2097168 | tf_op jit(solution)/shard_map/psum | solution.py:81
  220.6 3.6 %fusion.16 = f32[2,512,16]{1,2,0:T(8,128)S(1)} fusion(f32[2,512,512]{2,1,0:T(8,128)} %all-reduce.3.cloned.1.call-done, f32[512,16]{0,1:T(8,128)S(1)} %copy-done), kind=kOutput, calls=%fused_computation.28 | convolution fusion | flops 101187584 | bytes 2195456 | tf_op jit(solution)/shard_map/wcd,wdr->wcr/dot_general | solution.py:84
  224.5 3.1 %custom-call.16 = f32[2,16,16]{2,1,0:T(8,128)S(1)} custom-call(f32[2,16,16]{2,1,0:T(8,128)S(1)} %fusion.43), custom_call_target="Cholesky" | custom-call | tf_op jit(solution)/shard_map/jit(cholesky)/cholesky | solution.py:43
  227.8 2.5 custom-call.17
  230.6 3.5 %fusion.14 = f32[2,512,16]{1,2,0:T(8,128)S(1)} fusion(f32[2,512,16]{1,2,0:T(8,128)S(1)} %convolution_bitcast_fusion.6, f32[2,512,512]{2,1,0:T(8,128)} %all-reduce.3.cloned.1.call-done), kind=kOutput, calls=%fused_computation.26 | convolution fusion | flops 101187584 | bytes 2228224 | tf_op jit(solution)/shard_map/wcd,wdr->wcr/dot_general | solution.py:84
  234.4 2.9 %custom-call.18 = f32[2,16,16]{2,1,0:T(8,128)S(1)} custom-call(f32[2,16,16]{2,1,0:T(8,128)S(1)} %fusion.41), custom_call_target="Cholesky" | custom-call | tf_op jit(solution)/shard_map/jit(cholesky)/cholesky | solution.py:43
  242.5 2.9 %custom-call.20 = f32[2,16,16]{2,1,0:T(8,128)S(1)} custom-call(f32[2,16,16]{2,1,0:T(8,128)S(1)} %fusion.39), custom_call_target="Cholesky" | custom-call | tf_op jit(solution)/shard_map/jit(cholesky)/cholesky | solution.py:43
  250.7 2.9 %custom-call.22 = f32[2,16,16]{2,1,0:T(8,128)S(1)} custom-call(f32[2,16,16]{2,1,0:T(8,128)S(1)} %fusion.37), custom_call_target="Cholesky" | custom-call | tf_op jit(solution)/shard_map/jit(cholesky)/cholesky | solution.py:43
  258.8 2.9 %custom-call.24 = f32[2,16,16]{2,1,0:T(8,128)S(1)} custom-call(f32[2,16,16]{2,1,0:T(8,128)S(1)} %fusion.35), custom_call_target="Cholesky" | custom-call | tf_op jit(solution)/shard_map/jit(cholesky)/cholesky | solution.py:43
  266.9 2.9 %custom-call.26 = f32[2,16,16]{2,1,0:T(8,128)S(1)} custom-call(f32[2,16,16]{2,1,0:T(8,128)S(1)} %fusion.33), custom_call_target="Cholesky" | custom-call | tf_op jit(solution)/shard_map/jit(cholesky)/cholesky | solution.py:43
  270.1 2.6 custom-call.27
  273.0 5.3 %fusion = bf16[128,5120]{1,0:T(8,128)(2,1)} fusion(bf16[256,5120]{1,0:T(8,128)(2,1)} %copy-done.4, bf16[256,5120]{1,0:T(8,128)(2,1)} %copy-done.6, bf16[2,512,16]{1,2,0:T(8,128)(2,1)S(1)} %fusion.20), kind=kOutput, calls=%fused_computation.2 | convolution fusion | flops 117391360 | bytes 7884800 | tf_op jit(solution)/shard_map/dot_general | solution.py:93
  278.3 4.0 %fusion.1 = bf16[128,5120]{1,0:T(8,128)(2,1)} fusion(bf16[256,5120]{1,0:T(8,128)(2,1)S(1)} %copy-done.5, bf16[128,5120]{1,0:T(8,128)(2,1)} %copy-done.7, bf16[256,5120]{1,0:T(8,128)(2,1)} %copy-done.6, bf16[2,512,16]{1,2,0:T(8,128)(2,1)S(1)} %fusion.20), kind=kOutput, calls=%fused_computation.3 | convolution fusion | flops 122634240 | bytes 9195520 | tf_op jit(solution)/shard_map/dot_general | solution.py:93
  282.2 3.4 %pad_maximum_fusion.7 = bf16[256,5120]{1,0:T(8,128)(2,1)} fusion(bf16[128,5120]{1,0:T(8,128)(2,1)} %fusion.1, bf16[128,5120]{1,0:T(8,128)(2,1)} %fusion), kind=kLoop, calls=%fused_computation.14 | loop fusion | flops 5242880 | bytes 5242880 | tf_op jit(solution)/shard_map/concatenate | solution.py:99
  (107 shorter events, 38.7 us)
Async XLA Ops:
  6.5 214.0 %copy-start = (f32[512,16]{0,1:T(8,128)S(1)}, f32[512,16]{0,1:T(8,128)}, u32[]{:S(2)}) copy-start(f32[512,16]{0,1:T(8,128)} %param.8) | copy-start | bytes 98308
  6.5 15.7 %copy-start.2 = (bf16[256,5120]{1,0:T(8,128)(2,1)S(1)}, bf16[256,5120]{1,0:T(8,128)(2,1)}, u32[]{:S(2)}) copy-start(bf16[256,5120]{1,0:T(8,128)(2,1)} %param.6) | copy-start | bytes 7864324
  6.5 214.0 %all-reduce.3.cloned.1.call-start = ((), (), s32[]{:S(2)}) async-start(), calls=%async_computation | async-start | bytes 4194304 | tf_op jit(solution)/shard_map/psum | solution.py:81
  7.7 13.5 %collective-permute-start = (bf16[256,64]{1,0:T(8,128)(2,1)S(1)}, bf16[256,64]{1,0:T(8,128)(2,1)S(1)}, u32[]{:S(2)}, u32[]{:S(2)}) collective-permute-start(bf16[256,64]{1,0:T(8,128)(2,1)S(1)} %get-tuple-element.10), channel_id=1, source_target_pairs={{0,1},{1,2},{2,3},{4,5},{5,6},{6,7},{8,9},{9,10},{10,11},{12,13},{... | collective-permute-start | bytes 98312 | tf_op jit(solution)/shard_map/ppermute | solution.py:20
  17.9 9.5 %collective-permute-start.1 = (bf16[256,64]{1,0:T(8,128)(2,1)S(1)}, bf16[256,64]{1,0:T(8,128)(2,1)S(1)}, u32[]{:S(2)}, u32[]{:S(2)}) collective-permute-start(bf16[256,64]{1,0:T(8,128)(2,1)S(1)} %get-tuple-element.9), channel_id=1, source_target_pairs={{1,0},{2,1},{3,2},{5,4},{6,5},{7,6},{9,8},{10,9},{11,10},{13,12},{... | collective-permute-start | bytes 98312 | tf_op jit(solution)/shard_map/ppermute | solution.py:23
  29.1 2.3 copy-start.3
  31.5 17.2 %collective-permute-start.2 = (f32[4,5120]{1,0:T(4,128)S(1)}, f32[4,5120]{1,0:T(4,128)S(1)}, u32[]{:S(2)}, u32[]{:S(2)}) collective-permute-start(f32[4,5120]{1,0:T(4,128)S(1)} %bitcast.162), channel_id=1, source_target_pairs={{4,0},{8,4},{12,8},{16,12},{20,16},{24,20},{28,24},{32,28},{36,32}... | collective-permute-start | bytes 245768 | tf_op jit(solution)/shard_map/ppermute | solution.py:23
  32.8 15.9 %collective-permute-start.3 = (f32[4,5120]{1,0:T(4,128)S(1)}, f32[4,5120]{1,0:T(4,128)S(1)}, u32[]{:S(2)}, u32[]{:S(2)}) collective-permute-start(f32[4,5120]{1,0:T(4,128)S(1)} %bitcast.161), channel_id=1, source_target_pairs={{0,4},{4,8},{8,12},{12,16},{16,20},{20,24},{24,28},{28,32},{32,36}... | collective-permute-start | bytes 245768 | tf_op jit(solution)/shard_map/ppermute | solution.py:20
  53.3 57.4 %copy-start.4 = (bf16[256,5120]{1,0:T(8,128)(2,1)}, bf16[256,5120]{1,0:T(8,128)(2,1)S(1)}, u32[]{:S(2)}) copy-start(bf16[256,5120]{1,0:T(8,128)(2,1)S(1)} %fusion.3) | copy-start | bytes 7864324
  53.3 54.5 %collective-permute-start.4 = (bf16[256,5120]{1,0:T(8,128)(2,1)S(1)}, bf16[256,5120]{1,0:T(8,128)(2,1)S(1)}, u32[]{:S(2)}, u32[]{:S(2)}) collective-permute-start(bf16[256,5120]{1,0:T(8,128)(2,1)S(1)} %fusion.3), channel_id=1, source_target_pairs={{0,4},{4,8},{8,12},{12,16},{16,20},{20,24},{24,28},{28,32},{32,36}... | collective-permute-start | bytes 7864328 | tf_op jit(solution)/shard_map/ppermute | solution.py:31
  56.7 54.0 %collective-permute-start.5 = (bf16[128,5120]{1,0:T(8,128)(2,1)S(1)}, bf16[128,5120]{1,0:T(8,128)(2,1)S(1)}, u32[]{:S(2)}, u32[]{:S(2)}) collective-permute-start(bf16[128,5120]{1,0:T(8,128)(2,1)S(1)} %slice.168), channel_id=1, source_target_pairs={{4,0},{8,4},{12,8},{16,12},{20,16},{24,20},{28,24},{32,28},{36,32}... | collective-permute-start | bytes 3932168 | tf_op jit(solution)/shard_map/ppermute | solution.py:31
  107.8 2.9 %copy-start.6 = (bf16[256,5120]{1,0:T(8,128)(2,1)}, bf16[256,5120]{1,0:T(8,128)(2,1)S(1)}, u32[]{:S(2)}) copy-start(bf16[256,5120]{1,0:T(8,128)(2,1)S(1)} %collective-permute-done.4) | copy-start | bytes 7864324
  110.8 2.9 copy-start.7
  220.6 19.8 %copy-start.1 = (f32[2,512,512]{2,1,0:T(8,128)S(1)}, f32[2,512,512]{2,1,0:T(8,128)}, u32[]{:S(2)}) copy-start(f32[2,512,512]{2,1,0:T(8,128)} %all-reduce.3.cloned.1.call-done) | copy-start | bytes 6291460
  273.0 5.3 %copy-start.5 = (bf16[256,5120]{1,0:T(8,128)(2,1)S(1)}, bf16[256,5120]{1,0:T(8,128)(2,1)}, u32[]{:S(2)}) copy-start(bf16[256,5120]{1,0:T(8,128)(2,1)} %copy-done.4) | copy-start | bytes 7864324
Sparse Core Ops, SparseCore 0:
  115.4 105.1 all-reduce.2
where the time goes:
time: 293 us; the launch traced here: 292 us
  waiting for transfers between devices  158 us (54%)
  other arithmetic  45 us (15%)
  matrix products  34.3 us (12%)
  starting transfers between devices  22.2 us (8%)
  local copies, waits for them, and re-layouts  19.7 us (7%)
  between operations  13.8 us (5%)
    psum x1, waiting for transfers between devices, per_device(): scatter_mat = lax.psum(partial_mats, 'ta') / total_time  105 us
    ppermute x2, waiting for transfers between devices, shifted(): lax.ppermute(value, axis, [(source, source + steps) for source in range(f...  49.6 us
    another operation x19, other arithmetic, orthonormal(): lower = jnp.linalg.cholesky(gram)  18.7 us
    another operation x13, other arithmetic, orthonormal(): lax.linalg.triangular_solve(lower, image, left_side=False, lower=True, tr...  15.4 us
    dot_general x6, matrix products, per_device(): jnp.einsum('wcd,wdr->wcr', scatter_mat, basis, precision=lax.Precision.HI...  14.8 us
    ppermute x2, starting transfers between devices, with_halo(): lax.ppermute(lax.slice_in_dim(block, block.shape[dim] - width, None, axis...  14.2 us
    dot_general x2, matrix products, per_device(): jnp.dot(rounded[number, 2 * STRIDE:3 * STRIDE], coeffs, preferred_element...  9.23 us
    reshape x1, local copies, waits for them, and re-layouts, per_device(): filtered = jnp.einsum('bct,tu->cbu', pieces, band_matrix, preferred_eleme...  5.95 us
  transfers between devices with their start and end apart: 7, of which 3 were waited for; matrix products, arithmetic and copies ran while one was open for 7% of the time, Pallas kernels for 0%

commit v1 on v0

--- a/solution.py
+++ b/solution.py
@@ -10,6 +10,12 @@
 RANK = 16
 ITERS = 6
 WIN = 512
+
+
+def spans_balance(x0, comm_axis):
+    new = lax.all_gather(x0, axis_name=comm_axis)
+    right_arr = jnp.sum(new, axis=0)
+    return right_arr
 
 
 def with_halo(block, sides, width):
@@ -78,7 +84,7 @@
             for number in range(windows)
         ]
     )
-    scatter_mat = lax.psum(partial_mats, "ta") / total_time
+    scatter_mat = spans_balance(partial_mats, "ta") / total_time
     for sweep in range(ITERS):
         basis = orthonormal(
             jnp.einsum("wcd,wdr->wcr", scatter_mat, basis, precision=lax.Precision.HIGHEST)

time: 293 us -> 306 us (1.044)
  waiting for transfers between devices: 158 us -> 170 us
  other arithmetic: 45 us -> 49.6 us
  matrix products: 34.3 us -> 30.9 us
    all_gather x0 -> x1, waiting for transfers between devices: none -> 117 us  [spans_balance(): new = lax.all_gather(x0, axis_name=comm_axis)]
    psum x1 -> x0, waiting for transfers between devices: 105 us -> none  [per_device(): scatter_mat = lax.psum(partial_mats, 'ta') / total_time]
    reduce_sum x0 -> x1, other arithmetic: none -> 4.65 us  [spans_balance(): right_arr = jnp.sum(new, axis=0)]
    dot_general x6, matrix products: 14.8 us -> 11.4 us  [per_device(): jnp.einsum('wcd,wdr->wcr', scatter_mat, basis, precision=lax.Precision.HI...]
  transfers between devices with their start and end apart: 7 -> 7, of which waited for: 3 -> 3; matrix products, arithmetic and copies ran while one was open for 7% -> 6% of each run, Pallas kernels for 0% -> 0%
where the time goes in v1:
time: 306 us
  waiting for transfers between devices  170 us (56%)
  other arithmetic  49.6 us (16%)
  matrix products  30.9 us (10%)
  starting transfers between devices  22.2 us (7%)
  local copies, waits for them, and re-layouts  19.7 us (6%)
  between operations  13.8 us (5%)
    all_gather x1, waiting for transfers between devices, spans_balance(): new = lax.all_gather(x0, axis_name=comm_axis)  117 us
    ppermute x2, waiting for transfers between devices, shifted(): lax.ppermute(value, axis, [(source, source + steps) for source in range(f...  49.6 us
    another operation x19, other arithmetic, orthonormal(): lower = jnp.linalg.cholesky(gram)  18.7 us
    another operation x13, other arithmetic, orthonormal(): lax.linalg.triangular_solve(lower, image, left_side=False, lower=True, tr...  15.4 us
    ppermute x2, starting transfers between devices, with_halo(): lax.ppermute(lax.slice_in_dim(block, block.shape[dim] - width, None, axis...  14.2 us
    dot_general x6, matrix products, per_device(): jnp.einsum('wcd,wdr->wcr', scatter_mat, basis, precision=lax.Precision.HI...  11.4 us
    dot_general x2, matrix products, per_device(): jnp.dot(rounded[number, 2 * STRIDE:3 * STRIDE], coeffs, preferred_element...  9.18 us
  transfers between devices with their start and end apart: 7, of which 3 were waited for; matrix products, arithmetic and copies ran while one was open for 6% of the time, Pallas kernels for 0%

profile of v1, /device:TPU:1, one launch (start us, length us, event | category | flops | bytes accessed | tf_op | source)
XLA Modules:
  0.0 305.9 jit_solution(10482147368269803812)
XLA Ops:
  7.7 10.2 %collective-permute-start = (bf16[256,64]{1,0:T(8,128)(2,1)S(1)}, bf16[256,64]{1,0:T(8,128)(2,1)S(1)}, u32[]{:S(2)}, u32[]{:S(2)}) collective-permute-start(bf16[256,64]{1,0:T(8,128)(2,1)S(1)} %get-tuple-element.10), channel_id=1, source_target_pairs={{0,1},{1,2},{2,3},{4,5},{5,6},{6,7},{8,9},{9,10},{10,11},{12,13},{... | collective-permute-start | bytes 98312 | tf_op jit(solution)/shard_map/ppermute | solution.py:26
  24.8 2.6 collective-permute-done.1
  32.8 4.0 %collective-permute-start.3 = (f32[4,5120]{1,0:T(4,128)S(1)}, f32[4,5120]{1,0:T(4,128)S(1)}, u32[]{:S(2)}, u32[]{:S(2)}) collective-permute-start(f32[4,5120]{1,0:T(4,128)S(1)} %bitcast.163), channel_id=1, source_target_pairs={{0,4},{4,8},{8,12},{12,16},{16,20},{20,24},{24,28},{28,32},{32,36}... | collective-permute-start | bytes 245768 | tf_op jit(solution)/shard_map/ppermute | solution.py:26
  36.8 5.9 %copy.36 = f32[256,20,256]{0,2,1:T(8,128)} copy(f32[256,20,256]{2,0,1:T(8,128)} %copy-done.2) | data formatting | bytes 10485760 | tf_op jit(solution)/shard_map/bct,tu->cbu/transpose | solution.py:66
  42.7 5.9 %copy.37 = f32[256,5120]{1,0:T(8,128)} copy(f32[256,5120]{0,1:T(8,128)} %bitcast.161) | data formatting | bytes 10485760 | tf_op jit(solution)/shard_map/reshape | solution.py:68
  48.6 4.7 %fusion.3 = bf16[256,5120]{1,0:T(8,128)(2,1)S(1)} fusion(f32[256,5120]{1,0:T(8,128)} %copy.37, f32[4,5120]{1,0:T(4,128)S(1)} %collective-permute-done.3, f32[4,5120]{1,0:T(4,128)S(1)} %collective-permute-done.2), kind=kLoop, calls=%fused_computation.10 | loop fusion | flops 5242880 | bytes 8028160 | tf_op jit(solution)/shard_map/convert_element_type | solution.py:70
  53.3 3.3 %collective-permute-start.4 = (bf16[256,5120]{1,0:T(8,128)(2,1)S(1)}, bf16[256,5120]{1,0:T(8,128)(2,1)S(1)}, u32[]{:S(2)}, u32[]{:S(2)}) collective-permute-start(bf16[256,5120]{1,0:T(8,128)(2,1)S(1)} %fusion.3), channel_id=1, source_target_pairs={{0,4},{4,8},{8,12},{12,16},{16,20},{20,24},{24,28},{28,32},{32,36}... | collective-permute-start | bytes 7864328 | tf_op jit(solution)/shard_map/ppermute | solution.py:37
  58.2 49.6 %collective-permute-done.4 = bf16[256,5120]{1,0:T(8,128)(2,1)S(1)} collective-permute-done((bf16[256,5120]{1,0:T(8,128)(2,1)S(1)}, bf16[256,5120]{1,0:T(8,128)(2,1)S(1)}, u32[]{:S(2)}, u32[]{:S(2)}) %collective-permute-start.4) | collective-permute-done | bytes 2621472 | tf_op jit(solution)/shard_map/ppermute | solution.py:37
  107.8 2.9 fusion.19
  110.8 2.9 fusion.18
  115.3 117.4 %all-gather.3.cloned.1.call-done = f32[8,512,512]{2,1,0:T(8,128)} async-done(((f32[2,512,512]{2,1,0:T(8,128)}), f32[8,512,512]{2,1,0:T(8,128)}) %all-gather.3.cloned.1.call-update) | async-done | bytes 8388624 | tf_op jit(solution)/shard_map/all_gather | solution.py:16
  232.7 4.7 %reduce_sum.9 = f32[2,512,512]{2,1,0:T(8,128)S(1)} reduce(f32[4,2,512,512]{3,2,1,0:T(8,128)} %bitcast.162, f32[]{:T(128)} %constant.35.clone.1), dimensions={0}, to_apply=%region_0.0 | reduce | flops 1572864 | bytes 10485764 | tf_op jit(solution)/shard_map/reduce_sum | solution.py:17
  239.6 3.1 %custom-call.16 = f32[2,16,16]{2,1,0:T(8,128)S(1)} custom-call(f32[2,16,16]{2,1,0:T(8,128)S(1)} %fusion.43), custom_call_target="Cholesky" | custom-call | tf_op jit(solution)/shard_map/jit(cholesky)/cholesky | solution.py:49
  242.9 2.5 custom-call.17
  247.8 2.9 custom-call.18
  256.0 2.9 custom-call.20
  264.1 2.9 custom-call.22
  267.3 2.5 custom-call.23
  272.2 2.9 custom-call.24
  280.4 2.9 custom-call.26
  283.6 2.6 custom-call.27
  286.5 5.3 %fusion = bf16[128,5120]{1,0:T(8,128)(2,1)} fusion(bf16[256,5120]{1,0:T(8,128)(2,1)} %copy-done.3, bf16[256,5120]{1,0:T(8,128)(2,1)} %copy-done.5, bf16[2,512,16]{1,2,0:T(8,128)(2,1)S(1)} %fusion.20), kind=kOutput, calls=%fused_computation.2 | convolution fusion | flops 117391360 | bytes 7884800 | tf_op jit(solution)/shard_map/dot_general | solution.py:99
  291.7 3.9 %fusion.1 = bf16[128,5120]{1,0:T(8,128)(2,1)} fusion(bf16[256,5120]{1,0:T(8,128)(2,1)S(1)} %copy-done.4, bf16[128,5120]{1,0:T(8,128)(2,1)} %copy-done.6, bf16[256,5120]{1,0:T(8,128)(2,1)} %copy-done.5, bf16[2,512,16]{1,2,0:T(8,128)(2,1)S(1)} %fusion.20), kind=kOutput, calls=%fused_computation.3 | convolution fusion | flops 122634240 | bytes 9195520 | tf_op jit(solution)/shard_map/dot_general | solution.py:99
  295.6 3.4 %pad_maximum_fusion.7 = bf16[256,5120]{1,0:T(8,128)(2,1)} fusion(bf16[128,5120]{1,0:T(8,128)(2,1)} %fusion.1, bf16[128,5120]{1,0:T(8,128)(2,1)} %fusion), kind=kLoop, calls=%fused_computation.14 | loop fusion | flops 5242880 | bytes 5242880 | tf_op jit(solution)/shard_map/concatenate | solution.py:105
  (106 shorter events, 40.0 us)
Async XLA Ops:
  6.5 230.8 %copy-start = (f32[512,16]{0,1:T(8,128)S(1)}, f32[512,16]{0,1:T(8,128)}, u32[]{:S(2)}) copy-start(f32[512,16]{0,1:T(8,128)} %param.8) | copy-start | bytes 98308
  6.5 15.7 %copy-start.1 = (bf16[256,5120]{1,0:T(8,128)(2,1)S(1)}, bf16[256,5120]{1,0:T(8,128)(2,1)}, u32[]{:S(2)}) copy-start(bf16[256,5120]{1,0:T(8,128)(2,1)} %param.6) | copy-start | bytes 7864324
  6.5 226.2 %all-gather.3.cloned.1.call-start = ((), (), s32[]{:S(2)}) async-start(), calls=%async_computation | async-start | bytes 10485760 | tf_op jit(solution)/shard_map/all_gather | solution.py:16
  7.7 13.5 %collective-permute-start = (bf16[256,64]{1,0:T(8,128)(2,1)S(1)}, bf16[256,64]{1,0:T(8,128)(2,1)S(1)}, u32[]{:S(2)}, u32[]{:S(2)}) collective-permute-start(bf16[256,64]{1,0:T(8,128)(2,1)S(1)} %get-tuple-element.10), channel_id=1, source_target_pairs={{0,1},{1,2},{2,3},{4,5},{5,6},{6,7},{8,9},{9,10},{10,11},{12,13},{... | collective-permute-start | bytes 98312 | tf_op jit(solution)/shard_map/ppermute | solution.py:26
  17.9 9.5 %collective-permute-start.1 = (bf16[256,64]{1,0:T(8,128)(2,1)S(1)}, bf16[256,64]{1,0:T(8,128)(2,1)S(1)}, u32[]{:S(2)}, u32[]{:S(2)}) collective-permute-start(bf16[256,64]{1,0:T(8,128)(2,1)S(1)} %get-tuple-element.9), channel_id=1, source_target_pairs={{1,0},{2,1},{3,2},{5,4},{6,5},{7,6},{9,8},{10,9},{11,10},{13,12},{... | collective-permute-start | bytes 98312 | tf_op jit(solution)/shard_map/ppermute | solution.py:29
  29.1 2.3 copy-start.2
  31.5 17.2 %collective-permute-start.2 = (f32[4,5120]{1,0:T(4,128)S(1)}, f32[4,5120]{1,0:T(4,128)S(1)}, u32[]{:S(2)}, u32[]{:S(2)}) collective-permute-start(f32[4,5120]{1,0:T(4,128)S(1)} %bitcast.164), channel_id=1, source_target_pairs={{4,0},{8,4},{12,8},{16,12},{20,16},{24,20},{28,24},{32,28},{36,32}... | collective-permute-start | bytes 245768 | tf_op jit(solution)/shard_map/ppermute | solution.py:29
  32.8 15.9 %collective-permute-start.3 = (f32[4,5120]{1,0:T(4,128)S(1)}, f32[4,5120]{1,0:T(4,128)S(1)}, u32[]{:S(2)}, u32[]{:S(2)}) collective-permute-start(f32[4,5120]{1,0:T(4,128)S(1)} %bitcast.163), channel_id=1, source_target_pairs={{0,4},{4,8},{8,12},{12,16},{16,20},{20,24},{24,28},{28,32},{32,36}... | collective-permute-start | bytes 245768 | tf_op jit(solution)/shard_map/ppermute | solution.py:26
  53.3 57.4 %copy-start.3 = (bf16[256,5120]{1,0:T(8,128)(2,1)}, bf16[256,5120]{1,0:T(8,128)(2,1)S(1)}, u32[]{:S(2)}) copy-start(bf16[256,5120]{1,0:T(8,128)(2,1)S(1)} %fusion.3) | copy-start | bytes 7864324
  53.3 54.5 %collective-permute-start.4 = (bf16[256,5120]{1,0:T(8,128)(2,1)S(1)}, bf16[256,5120]{1,0:T(8,128)(2,1)S(1)}, u32[]{:S(2)}, u32[]{:S(2)}) collective-permute-start(bf16[256,5120]{1,0:T(8,128)(2,1)S(1)} %fusion.3), channel_id=1, source_target_pairs={{0,4},{4,8},{8,12},{12,16},{16,20},{20,24},{24,28},{28,32},{32,36}... | collective-permute-start | bytes 7864328 | tf_op jit(solution)/shard_map/ppermute | solution.py:37
  56.7 54.0 %collective-permute-start.5 = (bf16[128,5120]{1,0:T(8,128)(2,1)S(1)}, bf16[128,5120]{1,0:T(8,128)(2,1)S(1)}, u32[]{:S(2)}, u32[]{:S(2)}) collective-permute-start(bf16[128,5120]{1,0:T(8,128)(2,1)S(1)} %slice.168), channel_id=1, source_target_pairs={{4,0},{8,4},{12,8},{16,12},{20,16},{24,20},{28,24},{32,28},{36,32}... | collective-permute-start | bytes 3932168 | tf_op jit(solution)/shard_map/ppermute | solution.py:37
  107.8 2.9 copy-start.5
  110.8 2.9 copy-start.6
  286.4 5.3 %copy-start.4 = (bf16[256,5120]{1,0:T(8,128)(2,1)S(1)}, bf16[256,5120]{1,0:T(8,128)(2,1)}, u32[]{:S(2)}) copy-start(bf16[256,5120]{1,0:T(8,128)(2,1)} %copy-done.3) | copy-start | bytes 7864324
Sparse Core Ops, SparseCore 0:
  115.4 117.3 all-gather.2
